TPU v7x, 32 devices: a whole 2x2x4 slice. The times are simulated.
32 devices in a mesh: rep: 2 (over x), member: 4 (over y, core), tp: 4 (over z).
Axes of the slice: x: 2, y: 2, z: 4, core: 2. Of those that a mesh axis runs over, the one named last changes fastest.
Arguments:
- states: bfloat16 [4096, 1024], P(('rep', 'member', 'tp')), parts along dimension 0, may hold values from -6 to 6
- member_of: int32 [4096, 1], P(('rep', 'member', 'tp')), parts along dimension 0, may hold values from 0 to 1; in each aligned block of 128 rows (0 to 127, 128 to 255, ...) at most 128 rows name the same one
- place: int32 [4096], P(('rep', 'member', 'tp')), parts along dimension 0, may hold values from 0 to 2047, as said below
- norm_gain: float32 [2, 1024], replicated, may hold values from 0.5 to 2
- w_up: bfloat16 [4, 1024, 2048], P('member', None, 'tp'), may hold values from -0.1875 to 0.1875
- w_down: bfloat16 [4, 2048, 1024], P('member', 'tp'), may hold values from -0.09375 to 0.09375
- policy_gain: float32 [1024], replicated, may hold values from 0.5 to 2
- w_policy: bfloat16 [1024, 128], replicated, may hold values from -0.1875 to 0.1875
Outputs:
- imagined: bfloat16 [4096, 1024], P(('rep', 'member', 'tp')), parts along dimension 0
- action: bfloat16 [4096, 128], P(('rep', 'member', 'tp')), parts along dimension 0
There are 2 independent parts, one for each index of `rep`. A program takes and returns all parts, laid end to end along the dimension named above; an argument that names none is the same for every part. Nothing has to cross between parts.
Inputs may be any that keep to these rules, and one draw needn't show every extreme that they name: `member_of`: at most 128 of the rows of one device name any one member, and that count is reached on some device. `place`: A permutation of the 2048 learner positions; learner device k holds positions k * 128 to (k + 1) * 128 - 1, and the rows of each device go exactly 8 to every learner device.
All inputs are finite; a program needn't handle non-finite values.
Results may differ from a plain program's by a relative error of at most 0.0069.
Values may be sent and summed in bfloat16 or wider, within the bound.
No kernel may reach another device: no remote copies, remote signals or barrier semaphores. Data moves between devices by JAX's collectives and lax.ppermute only.
A program may use at most 128 MiB of HBM per device.

v0:
```python
import jax
import jax.numpy as jnp
from jax import lax
from jax.sharding import PartitionSpec as P


def from_partner(value, axis, distance):
    return lax.ppermute(value, axis, [(i, i ^ 1 << distance) for i in range(lax.axis_size(axis))])


def rms_scale(values, gain):
    mean_square = jnp.mean(values * values, axis=-1, keepdims=True)
    return values * lax.rsqrt(mean_square + 1e-06) * gain


def running_rank(member_hits):
    return jnp.sum((jnp.cumsum(member_hits, axis=0) - member_hits) * member_hits, axis=1)


def local(states, member_of, place, norm_gain, w_up, w_down, policy_gain, w_policy):
    n_member = lax.axis_size("member")
    n_tp = lax.axis_size("tp")
    n_dev = n_member * n_tp
    group_width = 2 * n_tp
    member_total = n_member // 2
    rows_here = states.shape[0]
    feature_width = states.shape[1]
    slot_count = 2 * rows_here // n_dev
    member = member_of[:, 0]
    member_hits = (member[:, None] == jnp.arange(member_total, dtype=jnp.int32)[None, :]).astype(
        jnp.int32
    )
    earlier = running_rank(member_hits)
    target = (member * group_width + earlier % group_width) * slot_count + earlier // group_width
    picker = (jnp.arange(n_dev * slot_count, dtype=jnp.int32)[:, None] == target[None, :]).astype(
        jnp.bfloat16
    )
    outgoing = jnp.dot(picker, states, preferred_element_type=jnp.float32).astype(jnp.bfloat16)
    arrived = lax.all_to_all(
        outgoing.reshape(n_dev, slot_count, feature_width),
        ("member", "tp"),
        split_axis=0,
        concat_axis=0,
        tiled=True,
    )
    arrived = arrived.reshape(n_dev * slot_count, feature_width)
    arrived_count = arrived.shape[0]
    own_member = lax.axis_index("member") // 2
    gain_here = lax.dynamic_index_in_dim(norm_gain, own_member, 0, keepdims=False)
    normed = rms_scale(arrived.astype(jnp.float32), gain_here).astype(jnp.bfloat16)
    partner_normed = from_partner(normed, "member", 0)
    both_rows = jnp.concatenate([normed, partner_normed], axis=0)
    up_local = w_up[0]
    down_local = w_down[0]
    hidden = jax.nn.gelu(
        jnp.dot(
            lax.all_gather(both_rows, "tp", axis=0, tiled=True),
            up_local,
            preferred_element_type=jnp.float32,
        )
    ).astype(jnp.bfloat16)
    half_change = lax.psum_scatter(
        jnp.dot(hidden, down_local, preferred_element_type=jnp.float32),
        "tp",
        scatter_dimension=0,
        tiled=True,
    )
    partner_part = from_partner(half_change[arrived_count:], "member", 0)
    change = half_change[:arrived_count] + partner_part
    predicted = (arrived.astype(jnp.float32) + change).astype(jnp.bfloat16)
    returned = lax.all_to_all(
        predicted.reshape(n_dev, slot_count, feature_width),
        ("member", "tp"),
        split_axis=0,
        concat_axis=0,
        tiled=True,
    )
    returned = returned.reshape(n_dev * slot_count, feature_width)
    own_rows = jnp.einsum("sr,sd->rd", picker, returned, preferred_element_type=jnp.float32).astype(
        jnp.bfloat16
    )
    per_learner = rows_here // n_dev
    learner = place // rows_here
    spot_index = place % rows_here
    learner_hits = (learner[:, None] == jnp.arange(n_dev, dtype=jnp.int32)[None, :]).astype(
        jnp.int32
    )
    lane_index = learner * per_learner + running_rank(learner_hits)
    placer = jnp.arange(rows_here, dtype=jnp.int32)[:, None] == lane_index[None, :]
    packed = jnp.dot(
        placer.astype(jnp.bfloat16), own_rows, preferred_element_type=jnp.float32
    ).astype(jnp.bfloat16)
    packed_spot = jnp.sum(placer.astype(jnp.int32) * spot_index[None, :], axis=1)
    arrivals, arrival_spots = (
        lax.all_to_all(
            packed.reshape(n_dev, per_learner, feature_width),
            ("member", "tp"),
            split_axis=0,
            concat_axis=0,
            tiled=True,
        ),
        lax.all_to_all(
            packed_spot.reshape(n_dev, per_learner),
            ("member", "tp"),
            split_axis=0,
            concat_axis=0,
            tiled=True,
        ),
    )
    arrivals = arrivals.reshape(rows_here, feature_width)
    arrival_spots = arrival_spots.reshape(rows_here)
    settle = (jnp.arange(rows_here, dtype=jnp.int32)[:, None] == arrival_spots[None, :]).astype(
        jnp.bfloat16
    )
    imagined = jnp.dot(settle, arrivals, preferred_element_type=jnp.float32).astype(jnp.bfloat16)
    policy_normed = rms_scale(imagined.astype(jnp.float32), policy_gain).astype(jnp.bfloat16)
    action = jnp.tanh(jnp.dot(policy_normed, w_policy, preferred_element_type=jnp.float32)).astype(
        jnp.bfloat16
    )
    return (imagined, action)


def solution(mesh):
    in_specs = (
        P(("rep", "member", "tp"), None),
        P(("rep", "member", "tp"), None),
        P(("rep", "member", "tp")),
        P(),
        P("member", None, "tp"),
        P("member", "tp", None),
        P(),
        P(),
    )
    out_specs = (P(("rep", "member", "tp"), None), P(("rep", "member", "tp"), None))
    return jax.shard_map(local, mesh=mesh, in_specs=in_specs, out_specs=out_specs, check_vma=False)
```

profile of v0, /device:TPU:0, one launch (start us, length us, event | category | flops | bytes accessed | tf_op | source)
XLA Modules:
  0.0 330.6 jit_solution(9997030250772812439)
XLA Ops:
  7.2 0.0 copy-start
  7.2 0.0 copy-start.2
  7.2 0.9 fusion.38
  8.1 0.2 reduce_window_sum.23
  8.3 0.8 select_reduce_fusion
  9.1 0.7 multiply_add_fusion
  9.8 2.0 convolution_convert_fusion
  11.8 7.4 %all-to-all-start.1 = ((bf16[16,16,1024]{2,1,0:T(8,128)(2,1)}), bf16[16,16,1024]{2,1,0:T(8,128)(2,1)S(1)}, u32[]{:S(2)}, u32[]{:S(2)}) async-start(bf16[16,16,1024]{2,1,0:T(8,128)(2,1)} %bitcast.2), calls=%async_computation.1 | async-start | bytes 1048576 | tf_op jit(solution)/shard_map/all_to_all | solution.py:39
  19.2 0.0 all-gather.2.cloned.1.call-start
  19.3 0.7 constant_dynamic-slice_fusion
  20.0 14.9 %all-to-all-done.1 = bf16[16,16,1024]{2,1,0:T(8,128)(2,1)S(1)} async-done(((bf16[16,16,1024]{2,1,0:T(8,128)(2,1)}), bf16[16,16,1024]{2,1,0:T(8,128)(2,1)S(1)}, u32[]{:S(2)}, u32[]{:S(2)}) %all-to-all-start.1) | async-done | bytes 524320 | tf_op jit(solution)/shard_map/all_to_all | solution.py:39
  34.9 0.2 fusion.25
  35.1 0.1 rsqrt.20
  35.1 0.2 fusion.27
  35.3 0.1 collective-permute-start
  35.4 1.9 collective-permute-done
  37.3 1.1 pad_maximum_fusion
  38.4 0.0 all-gather.2.cloned.1.call-update
  38.4 0.0 reduce-scatter.2.cloned.1.call-start
  38.5 79.5 %all-gather.2.cloned.1.call-done = bf16[2048,1024]{1,0:T(8,128)(2,1)} async-done(((bf16[512,1024]{1,0:T(8,128)(2,1)}), bf16[2048,1024]{1,0:T(8,128)(2,1)}) %all-gather.2.cloned.1.call-update) | async-done | bytes 4194320 | tf_op jit(solution)/shard_map/all_gather | solution.py:57
  118.0 0.0 copy-done
  118.0 10.6 %fusion.8 = f32[2048,1024]{1,0:T(8,128)} fusion(bf16[1,512,1024]{2,1,0:T(8,128)(2,1)S(1)} %copy-done, bf16[2048,1024]{1,0:T(8,128)(2,1)} %all-gather.2.cloned.1.call-done, bf16[1,1024,512]{2,1,0:T(8,128)(2,1)S(1)} %copy-done.2), kind=kOutput, calls=%fused_computation.9 | convolution fusion | flops 4304404480 | bytes 14680064 | tf_op jit(solution)/shard_map/dot_general | solution.py:63
  128.6 0.0 reduce-scatter.2.cloned.1.call-update
  128.6 0.0 copy-start.5
  128.6 0.0 copy-start.3
  128.6 0.0 copy-start.4
  128.7 143.1 %reduce-scatter.2.cloned.1.call-done = f32[512,1024]{1,0:T(8,128)} async-done(((f32[2048,1024]{1,0:T(8,128)}), f32[512,1024]{1,0:T(8,128)}) %reduce-scatter.2.cloned.1.call-update) | async-done | bytes 2097168 | tf_op jit(solution)/shard_map/reduce_scatter | solution.py:62
  271.8 1.3 slice.9
  273.1 0.1 collective-permute-start.1
  273.2 2.6 collective-permute-done.1
  275.9 2.2 fusion.17
  278.1 5.4 %all-to-all-start.2 = ((bf16[16,16,1024]{2,1,0:T(8,128)(2,1)}), bf16[16,16,1024]{2,1,0:T(8,128)(2,1)S(1)}, u32[]{:S(2)}, u32[]{:S(2)}) async-start(bf16[16,16,1024]{2,1,0:T(8,128)(2,1)} %bitcast.7), calls=%async_computation.3 | async-start | bytes 1048576 | tf_op jit(solution)/shard_map/all_to_all | solution.py:71
  283.5 0.1 fusion.39
  283.6 0.2 reduce_window_sum.22
  283.8 0.2 select_reduce_fusion.2
  284.0 0.1 select_reduce_fusion.1
  284.1 0.7 all_to_all.15
  284.8 14.4 %all-to-all-done.2 = bf16[16,16,1024]{2,1,0:T(8,128)(2,1)S(1)} async-done(((bf16[16,16,1024]{2,1,0:T(8,128)(2,1)}), bf16[16,16,1024]{2,1,0:T(8,128)(2,1)S(1)}, u32[]{:S(2)}, u32[]{:S(2)}) %all-to-all-start.2) | async-done | bytes 524320 | tf_op jit(solution)/shard_map/all_to_all | solution.py:71
  299.2 3.5 %all-to-all-start = ((s32[16,1,8]{2,1,0:T(1,128)}), s32[16,1,8]{2,1,0:T(1,128)S(1)}, u32[]{:S(2)}, u32[]{:S(2)}) async-start(s32[16,1,8]{2,1,0:T(1,128)} %bitcast), calls=%async_computation | async-start | bytes 16384 | tf_op jit(solution)/shard_map/all_to_all | solution.py:102
  302.7 1.1 fusion.14
  303.8 5.1 %all-to-all-done = s32[16,1,8]{2,1,0:T(1,128)S(1)} async-done(((s32[16,1,8]{2,1,0:T(1,128)}), s32[16,1,8]{2,1,0:T(1,128)S(1)}, u32[]{:S(2)}, u32[]{:S(2)}) %all-to-all-start) | async-done | bytes 544 | tf_op jit(solution)/shard_map/all_to_all | solution.py:102
  308.9 3.5 %all-to-all-start.3 = ((bf16[16,8,1024]{2,1,0:T(8,128)(2,1)}), bf16[16,8,1024]{2,1,0:T(8,128)(2,1)S(1)}, u32[]{:S(2)}, u32[]{:S(2)}) async-start(bf16[16,8,1024]{2,1,0:T(8,128)(2,1)} %fusion.14), calls=%async_computation.4 | async-start | bytes 524288 | tf_op jit(solution)/shard_map/all_to_all | solution.py:95
  312.5 0.5 broadcast.140
  313.0 0.7 reduce.4
  313.6 0.1 eq.77
  313.7 8.7 %all-to-all-done.3 = bf16[16,8,1024]{2,1,0:T(8,128)(2,1)S(1)} async-done(((bf16[16,8,1024]{2,1,0:T(8,128)(2,1)}), bf16[16,8,1024]{2,1,0:T(8,128)(2,1)S(1)}, u32[]{:S(2)}, u32[]{:S(2)}) %all-to-all-start.3) | async-done | bytes 262176 | tf_op jit(solution)/shard_map/all_to_all | solution.py:95
  322.5 0.3 fusion.28
  322.8 0.9 fusion.15
  (10 shorter events, 0.0 us)
Async XLA Ops:
  7.2 110.8 %copy-start = (bf16[1,512,1024]{2,1,0:T(8,128)(2,1)S(1)}, bf16[1,512,1024]{2,1,0:T(8,128)(2,1)}, u32[]{:S(2)}) copy-start(bf16[1,512,1024]{2,1,0:T(8,128)(2,1)} %param.13) | copy-start | bytes 3145732
  7.2 110.8 %copy-start.2 = (bf16[1,1024,512]{2,1,0:T(8,128)(2,1)S(1)}, bf16[1,1024,512]{2,1,0:T(8,128)(2,1)}, u32[]{:S(2)}) copy-start(bf16[1,1024,512]{2,1,0:T(8,128)(2,1)} %param.12) | copy-start | bytes 3145732
  11.8 23.1 %all-to-all-start.1 = ((bf16[16,16,1024]{2,1,0:T(8,128)(2,1)}), bf16[16,16,1024]{2,1,0:T(8,128)(2,1)S(1)}, u32[]{:S(2)}, u32[]{:S(2)}) async-start(bf16[16,16,1024]{2,1,0:T(8,128)(2,1)} %bitcast.2), calls=%async_computation.1 | async-start | bytes 1048576 | tf_op jit(solution)/shard_map/all_to_all | solution.py:39
  19.2 98.8 %all-gather.2.cloned.1.call-start = ((), (), s32[]{:S(2)}) async-start(), calls=%async_computation.5 | async-start | bytes 5242880 | tf_op jit(solution)/shard_map/all_gather | solution.py:57
  35.3 2.0 collective-permute-start
  38.4 233.4 %reduce-scatter.2.cloned.1.call-start = ((), (), s32[]{:S(2)}) async-start(), calls=%async_computation.6 | async-start | bytes 10485760 | tf_op jit(solution)/shard_map/reduce_scatter | solution.py:62
  128.6 154.9 %copy-start.5 = (s32[128]{0:T(128)S(1)}, s32[128]{0:T(128)}, u32[]{:S(2)}) copy-start(s32[128]{0:T(128)} %param.10) | copy-start | bytes 1540
  128.6 194.2 %copy-start.3 = (bf16[1024,128]{1,0:T(8,128)(2,1)S(1)}, bf16[1024,128]{1,0:T(8,128)(2,1)}, u32[]{:S(2)}) copy-start(bf16[1024,128]{1,0:T(8,128)(2,1)} %param.15) | copy-start | bytes 786436
  128.6 194.2 %copy-start.4 = (f32[1024]{0:T(1024)S(1)}, f32[1024]{0:T(1024)}, u32[]{:S(2)}) copy-start(f32[1024]{0:T(1024)} %param.14) | copy-start | bytes 12292
  273.1 2.7 collective-permute-start.1
  278.1 21.1 %all-to-all-start.2 = ((bf16[16,16,1024]{2,1,0:T(8,128)(2,1)}), bf16[16,16,1024]{2,1,0:T(8,128)(2,1)S(1)}, u32[]{:S(2)}, u32[]{:S(2)}) async-start(bf16[16,16,1024]{2,1,0:T(8,128)(2,1)} %bitcast.7), calls=%async_computation.3 | async-start | bytes 1048576 | tf_op jit(solution)/shard_map/all_to_all | solution.py:71
  299.2 9.7 %all-to-all-start = ((s32[16,1,8]{2,1,0:T(1,128)}), s32[16,1,8]{2,1,0:T(1,128)S(1)}, u32[]{:S(2)}, u32[]{:S(2)}) async-start(s32[16,1,8]{2,1,0:T(1,128)} %bitcast), calls=%async_computation | async-start | bytes 16384 | tf_op jit(solution)/shard_map/all_to_all | solution.py:102
  308.9 13.6 %all-to-all-start.3 = ((bf16[16,8,1024]{2,1,0:T(8,128)(2,1)}), bf16[16,8,1024]{2,1,0:T(8,128)(2,1)S(1)}, u32[]{:S(2)}, u32[]{:S(2)}) async-start(bf16[16,8,1024]{2,1,0:T(8,128)(2,1)} %fusion.14), calls=%async_computation.4 | async-start | bytes 524288 | tf_op jit(solution)/shard_map/all_to_all | solution.py:95
  322.8 1.0 copy-start.1
Sparse Core Ops, SparseCore 0:
  38.5 79.4 all-gather.1
  128.7 143.0 reduce-scatter.1
where the time goes:
time: 331 us
  waiting for transfers between devices  270 us (82%)
  starting transfers between devices  20 us (6%)
  matrix products  15 us (5%)
  between operations  14.3 us (4%)
  other arithmetic  7.45 us (2%)
  local copies, waits for them, and re-layouts  3.45 us (1%)
    reduce_scatter x1, waiting for transfers between devices, local(): lax.psum_scatter(jnp.dot(hidden, down_local, preferred_element_type=jnp.f...  143 us
    all_gather x1, waiting for transfers between devices, local(): lax.all_gather(both_rows, 'tp', axis=0, tiled=True)  79.5 us
    all_to_all x1, waiting for transfers between devices, local(): lax.all_to_all(outgoing.reshape(n_dev, slot_count, feature_width), ('memb...  14.9 us
    all_to_all x1, waiting for transfers between devices, local(): lax.all_to_all(predicted.reshape(n_dev, slot_count, feature_width), ('mem...  14.4 us
    dot_general x1, matrix products, local(): jnp.dot(hidden, down_local, preferred_element_type=jnp.float32)  10.6 us
    all_to_all x1, waiting for transfers between devices, local(): lax.all_to_all(packed.reshape(n_dev, per_learner, feature_width), ('membe...  8.74 us
    all_to_all x1, starting transfers between devices, local(): lax.all_to_all(outgoing.reshape(n_dev, slot_count, feature_width), ('memb...  7.39 us
  transfers between devices with their start and end apart: 8, of which 8 were waited for; matrix products, arithmetic and copies ran while one was open for 1% of the time, Pallas kernels for 0%

commit v1 on v0

--- a/solution.py
+++ b/solution.py
@@ -2,6 +2,28 @@
 import jax.numpy as jnp
 from jax import lax
 from jax.sharding import PartitionSpec as P
+from jax.lax import axis_index, axis_size, ppermute
+
+
+def apply_region(here_x, mesh_dim):
+    moved = axis_index(mesh_dim)
+    ready = axis_size(mesh_dim)
+    field_out, taken_in = (ready, moved)
+    carry_in = here_x.shape[0] // field_out
+    vec_out = list(here_x.shape)
+    vec_out[0] = carry_in
+    r2 = vec_out[0]
+    vec_out[0] = r2 * field_out
+    raw_out = jnp.zeros(vec_out, here_x.dtype)
+    for p in range(field_out):
+        block_next = lax.dynamic_slice_in_dim(here_x, (taken_in ^ p) * carry_in, carry_in, axis=0)
+        if p:
+            bank = []
+            for m in range(field_out):
+                bank.append((m, m ^ p))
+            block_next = ppermute(block_next, mesh_dim, bank)
+        raw_out = lax.dynamic_update_slice_in_dim(raw_out, block_next, (taken_in ^ p) * r2, axis=0)
+    return raw_out
 
 
 def from_partner(value, axis, distance):
@@ -36,13 +58,7 @@
         jnp.bfloat16
     )
     outgoing = jnp.dot(picker, states, preferred_element_type=jnp.float32).astype(jnp.bfloat16)
-    arrived = lax.all_to_all(
-        outgoing.reshape(n_dev, slot_count, feature_width),
-        ("member", "tp"),
-        split_axis=0,
-        concat_axis=0,
-        tiled=True,
-    )
+    arrived = apply_region(outgoing.reshape(n_dev, slot_count, feature_width), ("member", "tp"))
     arrived = arrived.reshape(n_dev * slot_count, feature_width)
     arrived_count = arrived.shape[0]
     own_member = lax.axis_index("member") // 2

time: 331 us -> 368 us (1.11)
  starting transfers between devices: 20 us -> 43.4 us
  waiting for transfers between devices: 270 us -> 284 us
    ppermute x0 -> x15, starting transfers between devices: none -> 30.8 us  [apply_region(): block_next = ppermute(block_next, mesh_dim, bank)]
    ppermute x0 -> x15, waiting for transfers between devices: none -> 26.1 us  [apply_region(): block_next = ppermute(block_next, mesh_dim, bank)]
    all_to_all x1 -> x0, waiting for transfers between devices: 14.9 us -> none  [local(): lax.all_to_all(outgoing.reshape(n_dev, slot_count, feature_width), ('memb...]
    all_to_all x1 -> x0, starting transfers between devices: 7.39 us -> none  [local(): lax.all_to_all(outgoing.reshape(n_dev, slot_count, feature_width), ('memb...]
  transfers between devices with their start and end apart: 8 -> 22, of which waited for: 8 -> 18; matrix products, arithmetic and copies ran while one was open for 1% -> 1% of each run, Pallas kernels for 0% -> 0%
where the time goes in v1:
time: 368 us
  waiting for transfers between devices  284 us (77%)
  starting transfers between devices  43.4 us (12%)
  between operations  14.5 us (4%)
  matrix products  14.2 us (4%)
  other arithmetic  7.47 us (2%)
  local copies, waits for them, and re-layouts  3.69 us (1%)
    reduce_scatter x1, waiting for transfers between devices, local(): lax.psum_scatter(jnp.dot(hidden, down_local, preferred_element_type=jnp.f...  143 us
    all_gather x1, waiting for transfers between devices, local(): lax.all_gather(both_rows, 'tp', axis=0, tiled=True)  82.3 us
    ppermute x15, starting transfers between devices, apply_region(): block_next = ppermute(block_next, mesh_dim, bank)  30.8 us
    ppermute x15, waiting for transfers between devices, apply_region(): block_next = ppermute(block_next, mesh_dim, bank)  26.1 us
    all_to_all x1, waiting for transfers between devices, local(): lax.all_to_all(predicted.reshape(n_dev, slot_count, feature_width), ('mem...  14.4 us
    dot_general x1, matrix products, local(): jnp.dot(hidden, down_local, preferred_element_type=jnp.float32)  10.6 us
    all_to_all x1, waiting for transfers between devices, local(): lax.all_to_all(packed.reshape(n_dev, per_learner, feature_width), ('membe...  8.74 us
  transfers between devices with their start and end apart: 22, of which 18 were waited for; matrix products, arithmetic and copies ran while one was open for 1% of the time, Pallas kernels for 0%

profile of v1, /device:TPU:0, one launch (start us, length us, event | category | flops | bytes accessed | tf_op | source)
XLA Modules:
  0.0 367.6 jit_solution(13228797325757676176)
XLA Ops:
  7.3 0.8 fusion.38
  8.3 0.9 select_reduce_fusion
  9.3 0.7 and_select_fusion.2
  10.0 1.2 convolution_convert_fusion
  11.4 5.5 %collective-permute-start.14 = (bf16[1,16,1024]{2,1,0:T(8,128)(2,1)S(1)}, bf16[1,16,1024]{2,1,0:T(8,128)(2,1)S(1)}, u32[]{:S(2)}, u32[]{:S(2)}) collective-permute-start(bf16[1,16,1024]{2,1,0:T(8,128)(2,1)S(1)} %get-tuple-element.2), channel_id=1, source_target_pairs={{0,15},{1,14},{2,13},{3,12},{4,11},{5,10},{6,9},{7,8},{8,7},{9,6},... | collective-permute-start | bytes 98312 | tf_op jit(solution)/shard_map/ppermute | solution.py:24
  16.9 1.4 collective-permute-start.12
  18.3 0.4 collective-permute-start.11
  18.7 1.4 collective-permute-start
  20.1 0.7 constant_dynamic-slice_fusion.15
  20.8 1.9 collective-permute-done
  22.7 2.7 collective-permute-start.1
  25.4 2.1 collective-permute-done.1
  27.6 3.9 %collective-permute-start.2 = (bf16[1,16,1024]{2,1,0:T(8,128)(2,1)S(1)}, bf16[1,16,1024]{2,1,0:T(8,128)(2,1)S(1)}, u32[]{:S(2)}, u32[]{:S(2)}) collective-permute-start(bf16[1,16,1024]{2,1,0:T(8,128)(2,1)S(1)} %get-tuple-element.14), channel_id=1, source_target_pairs={{0,3},{1,2},{2,1},{3,0},{4,7},{5,6},{6,5},{7,4},{8,11},{9,10},{10,... | collective-permute-start | bytes 98312 | tf_op jit(solution)/shard_map/ppermute | solution.py:24
  31.5 1.9 collective-permute-done.2
  33.4 1.2 collective-permute-done.3
  34.6 3.3 collective-permute-done.4
  37.9 2.4 collective-permute-start.5
  40.3 1.9 collective-permute-done.5
  42.2 4.1 %collective-permute-start.6 = (bf16[1,16,1024]{2,1,0:T(8,128)(2,1)S(1)}, bf16[1,16,1024]{2,1,0:T(8,128)(2,1)S(1)}, u32[]{:S(2)}, u32[]{:S(2)}) collective-permute-start(bf16[1,16,1024]{2,1,0:T(8,128)(2,1)S(1)} %get-tuple-element.10), channel_id=1, source_target_pairs={{0,7},{1,6},{2,5},{3,4},{4,3},{5,2},{6,1},{7,0},{8,15},{9,14},{10,... | collective-permute-start | bytes 98312 | tf_op jit(solution)/shard_map/ppermute | solution.py:24
  46.3 1.6 collective-permute-done.6
  47.9 1.5 collective-permute-start.7
  49.4 2.4 collective-permute-done.7
  51.8 0.3 collective-permute-start.8
  52.1 4.5 %collective-permute-done.8 = bf16[1,16,1024]{2,1,0:T(8,128)(2,1)S(1)} collective-permute-done((bf16[1,16,1024]{2,1,0:T(8,128)(2,1)S(1)}, bf16[1,16,1024]{2,1,0:T(8,128)(2,1)S(1)}, u32[]{:S(2)}, u32[]{:S(2)}) %collective-permute-start.8) | collective-permute-done | bytes 32800 | tf_op jit(solution)/shard_map/ppermute | solution.py:24
  56.7 2.4 collective-permute-start.9
  59.1 3.3 collective-permute-done.9
  62.4 4.8 %collective-permute-start.10 = (bf16[1,16,1024]{2,1,0:T(8,128)(2,1)S(1)}, bf16[1,16,1024]{2,1,0:T(8,128)(2,1)S(1)}, u32[]{:S(2)}, u32[]{:S(2)}) collective-permute-start(bf16[1,16,1024]{2,1,0:T(8,128)(2,1)S(1)} %get-tuple-element.6), channel_id=1, source_target_pairs={{0,11},{1,10},{2,9},{3,8},{4,15},{5,14},{6,13},{7,12},{8,3},{9,2},... | collective-permute-start | bytes 98312 | tf_op jit(solution)/shard_map/ppermute | solution.py:24
  67.1 1.9 collective-permute-done.10
  69.7 1.9 collective-permute-done.15
  71.6 1.0 pad_maximum_fusion
  72.7 82.3 %all-gather.2.cloned.1.call-done = bf16[2048,1024]{1,0:T(8,128)(2,1)} async-done(((bf16[512,1024]{1,0:T(8,128)(2,1)}), bf16[2048,1024]{1,0:T(8,128)(2,1)}) %all-gather.2.cloned.1.call-update) | async-done | bytes 4194320 | tf_op jit(solution)/shard_map/all_gather | solution.py:73
  155.0 10.6 %fusion.8 = f32[2048,1024]{1,0:T(8,128)} fusion(bf16[1,512,1024]{2,1,0:T(8,128)(2,1)S(1)} %copy-done, bf16[2048,1024]{1,0:T(8,128)(2,1)} %all-gather.2.cloned.1.call-done, bf16[1,1024,512]{2,1,0:T(8,128)(2,1)S(1)} %copy-done.2), kind=kOutput, calls=%fused_computation.9 | convolution fusion | flops 4304404480 | bytes 14680064 | tf_op jit(solution)/shard_map/dot_general | solution.py:79
  165.6 143.1 %reduce-scatter.2.cloned.1.call-done = f32[512,1024]{1,0:T(8,128)} async-done(((f32[2048,1024]{1,0:T(8,128)}), f32[512,1024]{1,0:T(8,128)}) %reduce-scatter.2.cloned.1.call-update) | async-done | bytes 2097168 | tf_op jit(solution)/shard_map/reduce_scatter | solution.py:78
  308.8 1.3 slice.9
  310.2 2.6 collective-permute-done.16
  312.8 2.2 fusion.17
  315.1 5.4 %all-to-all-start.1 = ((bf16[16,16,1024]{2,1,0:T(8,128)(2,1)}), bf16[16,16,1024]{2,1,0:T(8,128)(2,1)S(1)}, u32[]{:S(2)}, u32[]{:S(2)}) async-start(bf16[16,16,1024]{2,1,0:T(8,128)(2,1)} %bitcast.7), calls=%async_computation.2 | async-start | bytes 1048576 | tf_op jit(solution)/shard_map/all_to_all | solution.py:87
  321.1 0.7 all_to_all.12
  321.8 14.4 %all-to-all-done.1 = bf16[16,16,1024]{2,1,0:T(8,128)(2,1)S(1)} async-done(((bf16[16,16,1024]{2,1,0:T(8,128)(2,1)}), bf16[16,16,1024]{2,1,0:T(8,128)(2,1)S(1)}, u32[]{:S(2)}, u32[]{:S(2)}) %all-to-all-start.1) | async-done | bytes 524320 | tf_op jit(solution)/shard_map/all_to_all | solution.py:87
  336.2 3.5 all-to-all-start
  339.7 1.2 fusion.14
  340.8 5.1 %all-to-all-done = s32[16,1,8]{2,1,0:T(1,128)S(1)} async-done(((s32[16,1,8]{2,1,0:T(1,128)}), s32[16,1,8]{2,1,0:T(1,128)S(1)}, u32[]{:S(2)}, u32[]{:S(2)}) %all-to-all-start) | async-done | bytes 544 | tf_op jit(solution)/shard_map/all_to_all | solution.py:118
  345.9 3.5 all-to-all-start.2
  349.5 0.5 broadcast.145
  350.0 0.7 reduce.4
  350.7 8.7 %all-to-all-done.2 = bf16[16,8,1024]{2,1,0:T(8,128)(2,1)S(1)} async-done(((bf16[16,8,1024]{2,1,0:T(8,128)(2,1)}), bf16[16,8,1024]{2,1,0:T(8,128)(2,1)S(1)}, u32[]{:S(2)}, u32[]{:S(2)}) %all-to-all-start.2) | async-done | bytes 262176 | tf_op jit(solution)/shard_map/all_to_all | solution.py:111
  359.5 0.3 fusion.28
  359.8 0.9 fusion.15
  (52 shorter events, 1.8 us)
Async XLA Ops:
  7.2 147.8 %copy-start = (bf16[1,512,1024]{2,1,0:T(8,128)(2,1)S(1)}, bf16[1,512,1024]{2,1,0:T(8,128)(2,1)}, u32[]{:S(2)}) copy-start(bf16[1,512,1024]{2,1,0:T(8,128)(2,1)} %param.13) | copy-start | bytes 3145732
  7.2 147.8 %all-gather.2.cloned.1.call-start = ((), (), s32[]{:S(2)}) async-start(), calls=%async_computation.4 | async-start | bytes 5242880 | tf_op jit(solution)/shard_map/all_gather | solution.py:73
  8.1 146.9 %copy-start.2 = (bf16[1,1024,512]{2,1,0:T(8,128)(2,1)S(1)}, bf16[1,1024,512]{2,1,0:T(8,128)(2,1)}, u32[]{:S(2)}) copy-start(bf16[1,1024,512]{2,1,0:T(8,128)(2,1)} %param.12) | copy-start | bytes 3145732
  11.4 57.7 %collective-permute-start.14 = (bf16[1,16,1024]{2,1,0:T(8,128)(2,1)S(1)}, bf16[1,16,1024]{2,1,0:T(8,128)(2,1)S(1)}, u32[]{:S(2)}, u32[]{:S(2)}) collective-permute-start(bf16[1,16,1024]{2,1,0:T(8,128)(2,1)S(1)} %get-tuple-element.2), channel_id=1, source_target_pairs={{0,15},{1,14},{2,13},{3,12},{4,11},{5,10},{6,9},{7,8},{8,7},{9,6},... | collective-permute-start | bytes 98312 | tf_op jit(solution)/shard_map/ppermute | solution.py:24
  16.9 52.2 %collective-permute-start.13 = (bf16[1,16,1024]{2,1,0:T(8,128)(2,1)S(1)}, bf16[1,16,1024]{2,1,0:T(8,128)(2,1)S(1)}, u32[]{:S(2)}, u32[]{:S(2)}) collective-permute-start(bf16[1,16,1024]{2,1,0:T(8,128)(2,1)S(1)} %get-tuple-element.3), channel_id=1, source_target_pairs={{0,14},{1,15},{2,12},{3,13},{4,10},{5,11},{6,8},{7,9},{8,6},{9,7},... | collective-permute-start | bytes 98312 | tf_op jit(solution)/shard_map/ppermute | solution.py:24
  16.9 52.1 %collective-permute-start.12 = (bf16[1,16,1024]{2,1,0:T(8,128)(2,1)S(1)}, bf16[1,16,1024]{2,1,0:T(8,128)(2,1)S(1)}, u32[]{:S(2)}, u32[]{:S(2)}) collective-permute-start(bf16[1,16,1024]{2,1,0:T(8,128)(2,1)S(1)} %get-tuple-element.4), channel_id=1, source_target_pairs={{0,13},{1,12},{2,15},{3,14},{4,9},{5,8},{6,11},{7,10},{8,5},{9,4},... | collective-permute-start | bytes 98312 | tf_op jit(solution)/shard_map/ppermute | solution.py:24
  18.3 50.7 %collective-permute-start.11 = (bf16[1,16,1024]{2,1,0:T(8,128)(2,1)S(1)}, bf16[1,16,1024]{2,1,0:T(8,128)(2,1)S(1)}, u32[]{:S(2)}, u32[]{:S(2)}) collective-permute-start(bf16[1,16,1024]{2,1,0:T(8,128)(2,1)S(1)} %get-tuple-element.5), channel_id=1, source_target_pairs={{0,12},{1,13},{2,14},{3,15},{4,8},{5,9},{6,10},{7,11},{8,4},{9,5},... | collective-permute-start | bytes 98312 | tf_op jit(solution)/shard_map/ppermute | solution.py:24
  18.7 4.0 %collective-permute-start = (bf16[1,16,1024]{2,1,0:T(8,128)(2,1)S(1)}, bf16[1,16,1024]{2,1,0:T(8,128)(2,1)S(1)}, u32[]{:S(2)}, u32[]{:S(2)}) collective-permute-start(bf16[1,16,1024]{2,1,0:T(8,128)(2,1)S(1)} %get-tuple-element.16), channel_id=1, source_target_pairs={{0,1},{1,0},{2,3},{3,2},{4,5},{5,4},{6,7},{7,6},{8,9},{9,8},{10,11... | collective-permute-start | bytes 98312 | tf_op jit(solution)/shard_map/ppermute | solution.py:24
  22.7 4.8 %collective-permute-start.1 = (bf16[1,16,1024]{2,1,0:T(8,128)(2,1)S(1)}, bf16[1,16,1024]{2,1,0:T(8,128)(2,1)S(1)}, u32[]{:S(2)}, u32[]{:S(2)}) collective-permute-start(bf16[1,16,1024]{2,1,0:T(8,128)(2,1)S(1)} %get-tuple-element.15), channel_id=1, source_target_pairs={{0,2},{1,3},{2,0},{3,1},{4,6},{5,7},{6,4},{7,5},{8,10},{9,11},{10,... | collective-permute-start | bytes 98312 | tf_op jit(solution)/shard_map/ppermute | solution.py:24
  27.6 5.8 %collective-permute-start.2 = (bf16[1,16,1024]{2,1,0:T(8,128)(2,1)S(1)}, bf16[1,16,1024]{2,1,0:T(8,128)(2,1)S(1)}, u32[]{:S(2)}, u32[]{:S(2)}) collective-permute-start(bf16[1,16,1024]{2,1,0:T(8,128)(2,1)S(1)} %get-tuple-element.14), channel_id=1, source_target_pairs={{0,3},{1,2},{2,1},{3,0},{4,7},{5,6},{6,5},{7,4},{8,11},{9,10},{10,... | collective-permute-start | bytes 98312 | tf_op jit(solution)/shard_map/ppermute | solution.py:24
  33.4 1.2 collective-permute-start.3
  34.6 3.3 collective-permute-start.4
  37.9 4.2 %collective-permute-start.5 = (bf16[1,16,1024]{2,1,0:T(8,128)(2,1)S(1)}, bf16[1,16,1024]{2,1,0:T(8,128)(2,1)S(1)}, u32[]{:S(2)}, u32[]{:S(2)}) collective-permute-start(bf16[1,16,1024]{2,1,0:T(8,128)(2,1)S(1)} %get-tuple-element.11), channel_id=1, source_target_pairs={{0,6},{1,7},{2,4},{3,5},{4,2},{5,3},{6,0},{7,1},{8,14},{9,15},{10,... | collective-permute-start | bytes 98312 | tf_op jit(solution)/shard_map/ppermute | solution.py:24
  42.2 5.7 %collective-permute-start.6 = (bf16[1,16,1024]{2,1,0:T(8,128)(2,1)S(1)}, bf16[1,16,1024]{2,1,0:T(8,128)(2,1)S(1)}, u32[]{:S(2)}, u32[]{:S(2)}) collective-permute-start(bf16[1,16,1024]{2,1,0:T(8,128)(2,1)S(1)} %get-tuple-element.10), channel_id=1, source_target_pairs={{0,7},{1,6},{2,5},{3,4},{4,3},{5,2},{6,1},{7,0},{8,15},{9,14},{10,... | collective-permute-start | bytes 98312 | tf_op jit(solution)/shard_map/ppermute | solution.py:24
  47.9 3.9 %collective-permute-start.7 = (bf16[1,16,1024]{2,1,0:T(8,128)(2,1)S(1)}, bf16[1,16,1024]{2,1,0:T(8,128)(2,1)S(1)}, u32[]{:S(2)}, u32[]{:S(2)}) collective-permute-start(bf16[1,16,1024]{2,1,0:T(8,128)(2,1)S(1)} %get-tuple-element.9), channel_id=1, source_target_pairs={{0,8},{1,9},{2,10},{3,11},{4,12},{5,13},{6,14},{7,15},{8,0},{9,1},... | collective-permute-start | bytes 98312 | tf_op jit(solution)/shard_map/ppermute | solution.py:24
  51.8 4.8 %collective-permute-start.8 = (bf16[1,16,1024]{2,1,0:T(8,128)(2,1)S(1)}, bf16[1,16,1024]{2,1,0:T(8,128)(2,1)S(1)}, u32[]{:S(2)}, u32[]{:S(2)}) collective-permute-start(bf16[1,16,1024]{2,1,0:T(8,128)(2,1)S(1)} %get-tuple-element.8), channel_id=1, source_target_pairs={{0,9},{1,8},{2,11},{3,10},{4,13},{5,12},{6,15},{7,14},{8,1},{9,0},... | collective-permute-start | bytes 98312 | tf_op jit(solution)/shard_map/ppermute | solution.py:24
  56.7 5.7 %collective-permute-start.9 = (bf16[1,16,1024]{2,1,0:T(8,128)(2,1)S(1)}, bf16[1,16,1024]{2,1,0:T(8,128)(2,1)S(1)}, u32[]{:S(2)}, u32[]{:S(2)}) collective-permute-start(bf16[1,16,1024]{2,1,0:T(8,128)(2,1)S(1)} %get-tuple-element.7), channel_id=1, source_target_pairs={{0,10},{1,11},{2,8},{3,9},{4,14},{5,15},{6,12},{7,13},{8,2},{9,3},... | collective-permute-start | bytes 98312 | tf_op jit(solution)/shard_map/ppermute | solution.py:24
  62.4 6.7 %collective-permute-start.10 = (bf16[1,16,1024]{2,1,0:T(8,128)(2,1)S(1)}, bf16[1,16,1024]{2,1,0:T(8,128)(2,1)S(1)}, u32[]{:S(2)}, u32[]{:S(2)}) collective-permute-start(bf16[1,16,1024]{2,1,0:T(8,128)(2,1)S(1)} %get-tuple-element.6), channel_id=1, source_target_pairs={{0,11},{1,10},{2,9},{3,8},{4,15},{5,14},{6,13},{7,12},{8,3},{9,2},... | collective-permute-start | bytes 98312 | tf_op jit(solution)/shard_map/ppermute | solution.py:24
  69.6 2.0 collective-permute-start.15
  72.7 236.1 %reduce-scatter.2.cloned.1.call-start = ((), (), s32[]{:S(2)}) async-start(), calls=%async_computation.5 | async-start | bytes 10485760 | tf_op jit(solution)/shard_map/reduce_scatter | solution.py:78
  165.6 194.2 %copy-start.3 = (bf16[1024,128]{1,0:T(8,128)(2,1)S(1)}, bf16[1024,128]{1,0:T(8,128)(2,1)}, u32[]{:S(2)}) copy-start(bf16[1024,128]{1,0:T(8,128)(2,1)} %param.15) | copy-start | bytes 786436
  165.6 194.2 %copy-start.4 = (f32[1024]{0:T(1024)S(1)}, f32[1024]{0:T(1024)}, u32[]{:S(2)}) copy-start(f32[1024]{0:T(1024)} %param.14) | copy-start | bytes 12292
  310.1 2.7 collective-permute-start.16
  315.1 21.1 %all-to-all-start.1 = ((bf16[16,16,1024]{2,1,0:T(8,128)(2,1)}), bf16[16,16,1024]{2,1,0:T(8,128)(2,1)S(1)}, u32[]{:S(2)}, u32[]{:S(2)}) async-start(bf16[16,16,1024]{2,1,0:T(8,128)(2,1)} %bitcast.7), calls=%async_computation.2 | async-start | bytes 1048576 | tf_op jit(solution)/shard_map/all_to_all | solution.py:87
  336.2 9.7 %all-to-all-start = ((s32[16,1,8]{2,1,0:T(1,128)}), s32[16,1,8]{2,1,0:T(1,128)S(1)}, u32[]{:S(2)}, u32[]{:S(2)}) async-start(s32[16,1,8]{2,1,0:T(1,128)} %bitcast), calls=%async_computation | async-start | bytes 16384 | tf_op jit(solution)/shard_map/all_to_all | solution.py:118
  345.9 13.6 %all-to-all-start.2 = ((bf16[16,8,1024]{2,1,0:T(8,128)(2,1)}), bf16[16,8,1024]{2,1,0:T(8,128)(2,1)S(1)}, u32[]{:S(2)}, u32[]{:S(2)}) async-start(bf16[16,8,1024]{2,1,0:T(8,128)(2,1)} %fusion.14), calls=%async_computation.3 | async-start | bytes 524288 | tf_op jit(solution)/shard_map/all_to_all | solution.py:111
  359.8 1.0 copy-start.1
Sparse Core Ops, SparseCore 0:
  72.8 82.1 all-gather.1
  165.7 143.0 reduce-scatter.1
